TPU v7x, 128 devices: a whole 4x4x4 slice. The times are simulated.
128 devices in a mesh: row: 8 (over z_lo, y), col: 16 (over x, z_hi, core).
Axes of the slice: x: 4, y: 4, z: 4 (z_hi: 2, z_lo: 2; z = z_hi * 2 + z_lo), core: 2. Of those that a mesh axis runs over, the one named last changes fastest.
Arguments:
- tokens: bfloat16 [2048, 2304], P('row', 'col'), may hold values from -6 to 6
- gate_weight: bfloat16 [8, 2304, 5760], P(None, 'col', 'row'), may hold values from -0.125 to 0.125
- up_weight: bfloat16 [8, 2304, 5760], P(None, 'col', 'row'), may hold values from -0.125 to 0.125
- down_weight: bfloat16 [8, 5760, 2304], P(None, 'row', 'col'), may hold values from -0.078125 to 0.078125
- route_ids: int32 [2048, 2], replicated, may hold values from 0 to 7, all different within a row; in each aligned block of 2048 rows (0 to 2047, 2048 to 4095, ...) at most 1024 rows name the same one
- route_weight: float32 [2048, 2], replicated, may hold values from 0.2 to 1
- prefill_cache: bfloat16 [2, 2048, 16, 2304], P(None, ('row', 'col')), may hold values from -6 to 6
- dest_col: int32 [8, 16, 16], P('row'), may hold values from 0 to 15, as said below
- dest_slot: int32 [8, 16, 16], P('row'), may hold values from 0 to 15, as said below
- pages_used: int32 [8, 16], P('row'), may hold values from 4 to 16, as said below
Outputs:
- mixed: bfloat16 [2048, 2304], P('row', 'col')
- decode_cache: bfloat16 [2, 2048, 16, 2304], P(None, ('row', 'col'))
Inputs may be any that keep to these rules, and one draw needn't show every extreme that they name: `route_ids`: each token names two different experts; no expert is named by more than 1024 tokens, a bound that some block reaches. For every device (r, c), dest_col[r, c, :] names each col index exactly 1 times. For every r and col index c2, the page slots of row r with dest_col = c2 carry distinct dest_slot values, so they fill all 16 slots of device (r, c2). The live slots of a device are its first pages_used slots; some device has all 16 live.
All inputs are finite; a program needn't handle non-finite values.
Results may differ from a plain program's by a relative error of at most 0.03.
Values may be sent and summed in bfloat16 or wider, within the bound.
No kernel may reach another device: no remote copies, remote signals or barrier semaphores. Data moves between devices by JAX's collectives and lax.ppermute only.
A program may use at most 192 MiB of HBM per device.

v0:
```python
import jax
import jax.numpy as jnp
from jax import lax
from jax.sharding import PartitionSpec as P


def aligned_apply(slot_rows, weights):
    experts = weights.shape[0]
    shaped = slot_rows.reshape(experts, -1, slot_rows.shape[1])
    product = jnp.einsum("ecd,edf->ecf", shaped, weights, preferred_element_type=jnp.float32)
    return product.reshape(-1, weights.shape[2])


def move_pages(prefill_cache, dest_col, dest_slot, pages_used):
    col_devices = lax.axis_size("col")
    own_index = lax.axis_index("col")
    slot_count = prefill_cache.shape[1]
    per_peer = slot_count // col_devices
    dest_table = dest_col[0]
    targets = dest_slot[0]
    page_index = jnp.arange(slot_count, dtype=jnp.int32)
    same_dest = dest_table[:, :, None] == dest_table[:, None, :]
    earlier = page_index[None, :] < page_index[:, None]
    dest_rank = jnp.sum((same_dest & earlier[None]).astype(jnp.int32), axis=2)
    send_order = lax.dynamic_index_in_dim(
        dest_table * per_peer + dest_rank, own_index, 0, keepdims=False
    )
    inverse = jnp.zeros((slot_count,), jnp.int32).at[send_order].set(page_index)
    own_used = lax.dynamic_index_in_dim(pages_used[0], own_index, 0, keepdims=False)
    is_live = page_index < own_used
    masked_pages = jnp.where(
        is_live[None, :, None, None], prefill_cache, jnp.zeros((), prefill_cache.dtype)
    )
    received = lax.all_to_all(
        masked_pages[:, inverse], "col", split_axis=1, concat_axis=1, tiled=True
    )
    senders = jnp.arange(col_devices, dtype=jnp.int32)[:, None]
    arrival = jnp.where(dest_table == own_index, senders * per_peer + dest_rank, slot_count)
    slot_of_arrival = (
        jnp.zeros((slot_count + 1,), jnp.int32)
        .at[arrival.reshape(-1)]
        .set(targets.reshape(-1))[:slot_count]
    )
    source_of_slot = jnp.zeros((slot_count,), jnp.int32).at[slot_of_arrival].set(page_index)
    return received[:, source_of_slot]


def shards(
    tokens,
    gate_weight,
    up_weight,
    down_weight,
    route_ids,
    route_weight,
    prefill_cache,
    dest_col,
    dest_slot,
    pages_used,
):
    decode_cache = move_pages(prefill_cache, dest_col, dest_slot, pages_used)
    gathered = lax.all_gather(tokens, "row", axis=0, tiled=True)
    token_count = route_ids.shape[0]
    assignments = token_count * 2
    capacity = token_count // 2
    experts = gate_weight.shape[0]
    flat_expert = route_ids.reshape(-1)
    labels = jnp.arange(experts, dtype=jnp.int32)
    assign_index = jnp.arange(assignments, dtype=jnp.int32)
    paired = jnp.concatenate([gate_weight, up_weight], axis=2)
    onehot = (flat_expert[:, None] == labels[None, :]).astype(jnp.int32)
    position = jnp.sum(jnp.cumsum(onehot, axis=0) * onehot, axis=1) - 1
    slot_of_assign = flat_expert * capacity + position
    row_assign = (
        jnp.full((experts * capacity,), assignments, jnp.int32).at[slot_of_assign].set(assign_index)
    )
    row_token = row_assign // 2
    padded_tokens = jnp.concatenate(
        [gathered, jnp.zeros((1, gathered.shape[1]), gathered.dtype)], axis=0
    )
    slot_rows = padded_tokens[row_token]
    weights_flat = jnp.concatenate([route_weight.reshape(-1), jnp.zeros((1,), jnp.float32)])
    row_weight = weights_flat[row_assign]
    partial_sums = aligned_apply(slot_rows, paired)
    summed = lax.psum_scatter(
        partial_sums.astype(jnp.bfloat16), "col", scatter_dimension=0, tiled=True
    ).astype(jnp.float32)
    share_rows = summed.shape[0]
    hidden_width = gate_weight.shape[2]
    own_weight = lax.dynamic_slice_in_dim(
        row_weight, lax.axis_index("col") * share_rows, share_rows, 0
    )
    hidden = (
        own_weight[:, None] * jax.nn.silu(summed[:, :hidden_width]) * summed[:, hidden_width:]
    ).astype(jnp.bfloat16)
    hidden_all = lax.all_gather(hidden, "col", axis=0, tiled=True)
    down_rows = aligned_apply(hidden_all, down_weight)
    pair_slots = slot_of_assign.reshape(token_count, 2)
    per_token = down_rows[pair_slots[:, 0]] + down_rows[pair_slots[:, 1]]
    mixed = lax.psum_scatter(per_token.astype(jnp.bfloat16), "row", scatter_dimension=0, tiled=True)
    return (mixed, decode_cache)


def solution(mesh):
    in_specs = (
        P("row", "col"),
        P(None, "col", "row"),
        P(None, "col", "row"),
        P(None, "row", "col"),
        P(),
        P(),
        P(None, ("row", "col"), None, None),
        P("row", None, None),
        P("row", None, None),
        P("row", None),
    )
    out_specs = (P("row", "col"), P(None, ("row", "col"), None, None))
    return jax.shard_map(shards, mesh=mesh, in_specs=in_specs, out_specs=out_specs, check_vma=False)
```

profile of v0, /device:TPU:0, one launch (start us, length us, event | category | flops | bytes accessed | tf_op | source)
XLA Modules:
  0.0 519.4 jit_solution(9502357657079924522)
XLA Ops:
  7.2 1.2 copy.43
  9.4 2.3 reduce-window.6
  12.4 2.0 sub.17
  14.4 2.8 fusion.28
  17.2 1.8 mul.40
  19.1 15.5 %scatter_custom_fusion = s32[8192]{0:T(1024)S(1)} fusion(s32[4096]{0:T(1024)S(1)} %bitcast.51, s32[4096]{0:T(1024)S(1)} %iota.35, s32[]{:T(128)} %constant.20.clone.1), kind=kCustom, calls=%fused_computation.48 | custom fusion | bytes 32772 | tf_op jit(solution)/shard_map/scatter | solution.py:74
  34.8 31.4 %all_gather.6 = bf16[2048,144]{1,0:T(8,128)(2,1)S(1)} all-gather(bf16[256,144]{1,0:T(8,128)(2,1)S(1)} %copy.46), channel_id=1, replica_groups=mesh['row'=8,'col'=16] {'row'}, dimensions={0}, use_global_device_ids=true | all-gather | bytes 663552 | tf_op jit(solution)/shard_map/all_gather | solution.py:61
  66.4 32.9 %gather_fusion.1 = bf16[8192,144]{1,0:T(8,128)(2,1)} fusion(bf16[2049,144]{1,0:T(8,128)(2,1)S(1)} %concatenate.10, s32[8192]{0:T(1024)S(1)} %get-tuple-element.15), kind=kCustom, calls=%fused_computation.1 | custom fusion | bytes 4751360 | tf_op jit(solution)/shard_map/gather | solution.py:80
  99.3 15.6 %convert_bitcast_fusion = bf16[8,180,8,1024]{3,2,1,0:T(8,128)(2,1)} fusion(bf16[8,1024,144]{2,1,0:T(8,128)(2,1)} %bitcast.44, bf16[8,144,720]{2,1,0:T(8,128)(2,1)} %param.12, bf16[8,144,720]{2,1,0:T(8,128)(2,1)} %param.11), kind=kOutput, calls=%fused_computation.10 | convolution fusion | flops 3415818240 | bytes 29270016 | tf_op jit(solution)/shard_map/ecd,edf->ecf/dot_general | solution.py:10
  114.9 20.1 %copy.60 = bf16[8,180,8,1024]{3,2,0,1:T(8,128)(2,1)} copy(bf16[8,180,8,1024]{3,2,1,0:T(8,128)(2,1)} %convert_bitcast_fusion) | data formatting | bytes 47185920 | tf_op jit(solution)/shard_map/convert_element_type | solution.py:85
  135.0 0.6 copy-done.4
  136.5 45.5 %gather_fusion = f32[8192]{0:T(1024)S(1)} fusion(f32[4097]{0:T(1024)S(1)} %pad_maximum_fusion, s32[8192]{0:T(1024)S(1)} %get-tuple-element.14), kind=kCustom, calls=%fused_computation | custom fusion | bytes 98304 | tf_op jit(solution)/shard_map/gather | solution.py:82
  182.2 135.9 %reduce-scatter.3.cloned.1.call-done = bf16[512,1440]{0,1:T(8,128)(2,1)} async-done(((bf16[8192,1440]{0,1:T(8,128)(2,1)}), bf16[512,1440]{0,1:T(8,128)(2,1)}) %reduce-scatter.3.cloned.1.call-update) | async-done | bytes 1474576 | tf_op jit(solution)/shard_map/reduce_scatter | solution.py:84
  318.0 1.8 convert_element_type.26
  319.9 1.4 fusion.6
  322.6 0.6 scatter_custom_fusion.1
  323.2 1.6 scatter_custom_fusion.2
  324.8 0.7 iota_compare_fusion.3
  325.5 3.3 broadcast_select_fusion
  328.8 3.9 gather_fusion.4
  332.7 4.6 all-to-all-start
  337.4 0.9 fusion.8
  338.3 96.2 %all-gather.2.cloned.1.call-done = bf16[8192,720]{0,1:T(8,128)(2,1)} async-done(((bf16[512,720]{0,1:T(8,128)(2,1)}), bf16[8192,720]{0,1:T(8,128)(2,1)}) %all-gather.2.cloned.1.call-update) | async-done | bytes 11796496 | tf_op jit(solution)/shard_map/all_gather | solution.py:95
  434.5 11.5 %fusion = f32[8,1024,144]{2,1,0:T(8,128)} fusion(bf16[8,720,144]{1,2,0:T(8,128)(2,1)S(1)} %copy-done, bf16[90,8,8,1024]{3,2,1,0:T(8,128)(2,1)} %bitcast.53), kind=kOutput, calls=%fused_computation.11 | convolution fusion | flops 1698693120 | bytes 18173952 | tf_op jit(solution)/shard_map/reshape | solution.py:11
  446.0 11.9 %gather_fusion.3 = f32[2048,144]{1,0:T(8,128)} fusion(f32[8192,144]{1,0:T(8,128)} %bitcast.41, s32[2048]{0:T(1024)S(1)} %get-tuple-element.18), kind=kCustom, calls=%fused_computation.3 | custom fusion | bytes 2367488 | tf_op jit(solution)/shard_map/gather | solution.py:98
  458.0 12.0 %gather_fusion.2 = f32[2048,144]{1,0:T(8,128)} fusion(f32[8192,144]{1,0:T(8,128)} %bitcast.42, s32[2048]{0:T(1024)S(1)} %get-tuple-element.19), kind=kCustom, calls=%fused_computation.2 | custom fusion | bytes 2367488 | tf_op jit(solution)/shard_map/gather | solution.py:98
  469.9 3.4 add_convert_fusion
  474.0 3.2 copy.53
  477.3 3.8 gather_fusion.5
  481.1 3.2 copy.55
  484.3 26.9 %reduce-scatter.5.cloned.1.call-done = bf16[256,144]{1,0:T(8,128)(2,1)} async-done(((bf16[2048,144]{1,0:T(8,128)(2,1)}), bf16[256,144]{1,0:T(8,128)(2,1)}) %reduce-scatter.5.cloned.1.call-update) | async-done | bytes 73744 | tf_op jit(solution)/shard_map/reduce_scatter | solution.py:99
  511.2 1.6 copy.54
  (55 shorter events, 5.1 us)
Async XLA Ops:
  7.2 427.3 %copy-start = (bf16[8,720,144]{1,2,0:T(8,128)(2,1)S(1)}, bf16[8,720,144]{1,2,0:T(8,128)(2,1)}, u32[]{:S(2)}) copy-start(bf16[8,720,144]{1,2,0:T(8,128)(2,1)} %param.13) | copy-start | bytes 4976644
  7.2 310.9 %reduce-scatter.3.cloned.1.call-start = ((), (), s32[]{:S(2)}) async-start(), calls=%async_computation.3 | async-start | bytes 25067520 | tf_op jit(solution)/shard_map/reduce_scatter | solution.py:84
  14.4 20.3 %copy-start.3 = (bf16[256,144]{0,1:T(8,128)(2,1)S(1)}, bf16[256,144]{0,1:T(8,128)(2,1)}, u32[]{:S(2)}) copy-start(bf16[256,144]{0,1:T(8,128)(2,1)} %param.10) | copy-start | bytes 221188
  135.0 0.7 copy-start.4
  135.0 299.5 %all-gather.2.cloned.1.call-start = ((), (), s32[]{:S(2)}) async-start(), calls=%async_computation.4 | async-start | bytes 12533760 | tf_op jit(solution)/shard_map/all_gather | solution.py:95
  319.8 1.4 copy-start.2
  319.8 2.1 copy-start.5
  319.8 2.1 copy-start.6
  332.7 4.6 copy-start.1
  332.7 141.3 %all-to-all-start = ((bf16[2,16,16,2304]{3,2,0,1:T(8,128)(2,1)}), bf16[2,16,16,2304]{3,2,0,1:T(8,128)(2,1)}, u32[]{:S(2)}, u32[]{:S(2)}) async-start(bf16[2,16,16,2304]{3,2,0,1:T(8,128)(2,1)} %bitcast.45), calls=%async_computation.2 | async-start | bytes 4718592 | tf_op jit(solution)/shard_map/all_to_all | solution.py:34
  337.3 173.9 %reduce-scatter.5.cloned.1.call-start = ((), (), s32[]{:S(2)}) async-start(), calls=%async_computation.5 | async-start | bytes 1179648 | tf_op jit(solution)/shard_map/reduce_scatter | solution.py:99
Sparse Core Ops, SparseCore 0:
  135.1 182.8 reduce-scatter.2
  321.4 113.0 all-gather.1
  473.5 37.7 reduce-scatter.4
where the time goes:
time: 520 us; the launch traced here: 519 us
  waiting for transfers between devices  259 us (50%)
  local copies, waits for them, and re-layouts  166 us (32%)
  blocking collectives  31.4 us (6%)
  matrix products  27.1 us (5%)
  other arithmetic  17.4 us (3%)
  between operations  14.1 us (3%)
    reduce_scatter x1, waiting for transfers between devices, shards(): lax.psum_scatter(partial_sums.astype(jnp.bfloat16), 'col', scatter_dimens...  136 us
    all_gather x1, waiting for transfers between devices, shards(): hidden_all = lax.all_gather(hidden, 'col', axis=0, tiled=True)  96.2 us
    gather x1, local copies, waits for them, and re-layouts, shards(): row_weight = weights_flat[row_assign]  45.5 us
    gather x1, local copies, waits for them, and re-layouts, shards(): slot_rows = padded_tokens[row_token]  32.9 us
    all_gather x1, blocking collectives, shards(): gathered = lax.all_gather(tokens, 'row', axis=0, tiled=True)  31.4 us
    reduce_scatter x1, waiting for transfers between devices, shards(): lax.psum_scatter(per_token.astype(jnp.bfloat16), 'row', scatter_dimension...  26.9 us
    gather x2, local copies, waits for them, and re-layouts, shards(): per_token = down_rows[pair_slots[:, 0]] + down_rows[pair_slots[:, 1]]  23.9 us
    convert_element_type x1, local copies, waits for them, and re-layouts, shards(): partial_sums.astype(jnp.bfloat16)  20.1 us
  transfers between devices with their start and end apart: 4, of which 3 were waited for; matrix products, arithmetic and copies ran while one was open for 21% of the time, Pallas kernels for 0%

commit v1 on v0

--- a/solution.py
+++ b/solution.py
@@ -92,7 +92,9 @@
     hidden = (
         own_weight[:, None] * jax.nn.silu(summed[:, :hidden_width]) * summed[:, hidden_width:]
     ).astype(jnp.bfloat16)
-    hidden_all = lax.all_gather(hidden, "col", axis=0, tiled=True)
+    hidden_all = jnp.concatenate(
+        lax.all_to_all(jnp.stack([hidden] * lax.axis_size("col")), "col", 0, 0), axis=0
+    )
     down_rows = aligned_apply(hidden_all, down_weight)
     pair_slots = slot_of_assign.reshape(token_count, 2)
     per_token = down_rows[pair_slots[:, 0]] + down_rows[pair_slots[:, 1]]

time: 520 us -> 663 us (1.27)
  waiting for transfers between devices: 259 us -> 341 us
  local copies, waits for them, and re-layouts: 166 us -> 209 us
  matrix products: 27.1 us -> 37.3 us
  starting transfers between devices: 4.7 us -> 12.7 us
    all_to_all x0 -> x1, waiting for transfers between devices: none -> 175 us  [shards(): lax.all_to_all(jnp.stack([hidden] * lax.axis_size('col')), 'col', 0, 0)]
    all_gather x1 -> x0, waiting for transfers between devices: 96.2 us -> none  [shards(): hidden_all = lax.all_gather(hidden, 'col', axis=0, tiled=True)]
    another operation x0 -> x2, local copies, waits for them, and re-layouts: none -> 23.4 us  [the longest x1 18 us: aligned_apply(): shaped = slot_rows.reshape(experts, -1, slot_rows.shape[1])]
    all_to_all x0 -> x1, local copies, waits for them, and re-layouts: none -> 19.8 us  [shards(): lax.all_to_all(jnp.stack([hidden] * lax.axis_size('col')), 'col', 0, 0)]
    reshape x1, matrix products: 11.5 us -> 21.7 us  [aligned_apply(): return product.reshape(-1, weights.shape[2])]
  transfers between devices with their start and end apart: 4 -> 4, of which waited for: 3 -> 3; matrix products, arithmetic and copies ran while one was open for 21% -> 24% of each run, Pallas kernels for 0% -> 0%
where the time goes in v1:
time: 663 us; the launch traced here: 662 us
  waiting for transfers between devices  341 us (51%)
  local copies, waits for them, and re-layouts  209 us (32%)
  matrix products  37.3 us (6%)
  blocking collectives  31.4 us (5%)
  other arithmetic  16.6 us (3%)
  between operations  14.3 us (2%)
  starting transfers between devices  12.7 us (2%)
    all_to_all x1, waiting for transfers between devices, shards(): lax.all_to_all(jnp.stack([hidden] * lax.axis_size('col')), 'col', 0, 0)  175 us
    reduce_scatter x1, waiting for transfers between devices, shards(): lax.psum_scatter(partial_sums.astype(jnp.bfloat16), 'col', scatter_dimens...  136 us
    gather x1, local copies, waits for them, and re-layouts, shards(): row_weight = weights_flat[row_assign]  45.5 us
    gather x1, local copies, waits for them, and re-layouts, shards(): slot_rows = padded_tokens[row_token]  32.9 us
    all_gather x1, blocking collectives, shards(): gathered = lax.all_gather(tokens, 'row', axis=0, tiled=True)  31.4 us
    reduce_scatter x1, waiting for transfers between devices, shards(): lax.psum_scatter(per_token.astype(jnp.bfloat16), 'row', scatter_dimension...  30.3 us
    gather x2, local copies, waits for them, and re-layouts, shards(): per_token = down_rows[pair_slots[:, 0]] + down_rows[pair_slots[:, 1]]  23.9 us
    reshape x1, matrix products, aligned_apply(): return product.reshape(-1, weights.shape[2])  21.7 us
  transfers between devices with their start and end apart: 4, of which 3 were waited for; matrix products, arithmetic and copies ran while one was open for 24% of the time, Pallas kernels for 0%

profile of v1, /device:TPU:0, one launch (start us, length us, event | category | flops | bytes accessed | tf_op | source)
XLA Modules:
  0.0 662.1 jit_solution(16806648994632972437)
XLA Ops:
  7.2 1.2 copy.58
  9.4 2.3 reduce-window.6
  12.4 2.0 sub.17
  14.4 2.8 fusion.27
  17.2 1.8 mul.40
  19.1 15.5 %scatter_custom_fusion = s32[8192]{0:T(1024)S(1)} fusion(s32[4096]{0:T(1024)S(1)} %bitcast.49, s32[4096]{0:T(1024)S(1)} %iota.35, s32[]{:T(128)} %constant.20.clone.1), kind=kCustom, calls=%fused_computation.47 | custom fusion | bytes 32772 | tf_op jit(solution)/shard_map/scatter | solution.py:74
  34.8 31.4 %all_gather.3 = bf16[2048,144]{1,0:T(8,128)(2,1)S(1)} all-gather(bf16[256,144]{1,0:T(8,128)(2,1)S(1)} %copy.61), channel_id=1, replica_groups=mesh['row'=8,'col'=16] {'row'}, dimensions={0}, use_global_device_ids=true | all-gather | bytes 663552 | tf_op jit(solution)/shard_map/all_gather | solution.py:61
  66.4 32.9 %gather_fusion.1 = bf16[8192,144]{1,0:T(8,128)(2,1)} fusion(bf16[2049,144]{1,0:T(8,128)(2,1)S(1)} %concatenate.10, s32[8192]{0:T(1024)S(1)} %get-tuple-element.17), kind=kCustom, calls=%fused_computation.1 | custom fusion | bytes 4751360 | tf_op jit(solution)/shard_map/gather | solution.py:80
  99.3 15.6 %convert_bitcast_fusion = bf16[8,180,8,1024]{3,2,1,0:T(8,128)(2,1)} fusion(bf16[8,1024,144]{2,1,0:T(8,128)(2,1)} %bitcast.42, bf16[8,144,720]{2,1,0:T(8,128)(2,1)} %param.12, bf16[8,144,720]{2,1,0:T(8,128)(2,1)} %param.11), kind=kOutput, calls=%fused_computation.10 | convolution fusion | flops 3415818240 | bytes 29270016 | tf_op jit(solution)/shard_map/ecd,edf->ecf/dot_general | solution.py:10
  114.9 20.1 %copy.75 = bf16[8,180,8,1024]{3,2,0,1:T(8,128)(2,1)} copy(bf16[8,180,8,1024]{3,2,1,0:T(8,128)(2,1)} %convert_bitcast_fusion) | data formatting | bytes 47185920 | tf_op jit(solution)/shard_map/convert_element_type | solution.py:85
  136.5 45.5 %gather_fusion = f32[8192]{0:T(1024)S(1)} fusion(f32[4097]{0:T(1024)S(1)} %pad_maximum_fusion, s32[8192]{0:T(1024)S(1)} %get-tuple-element.16), kind=kCustom, calls=%fused_computation | custom fusion | bytes 98304 | tf_op jit(solution)/shard_map/gather | solution.py:82
  182.2 135.9 %reduce-scatter.3.cloned.1.call-done = bf16[512,1440]{0,1:T(8,128)(2,1)} async-done(((bf16[8192,1440]{0,1:T(8,128)(2,1)}), bf16[512,1440]{0,1:T(8,128)(2,1)}) %reduce-scatter.3.cloned.1.call-update) | async-done | bytes 1474576 | tf_op jit(solution)/shard_map/reduce_scatter | solution.py:84
  318.0 1.8 convert_element_type.26
  320.3 5.4 stack.2
  325.7 5.0 all-to-all-start
  332.9 1.4 scatter_custom_fusion.2
  335.0 3.3 broadcast_select_fusion
  338.3 3.9 gather_fusion.4
  342.3 0.9 fusion.7
  343.2 174.6 %all-to-all-done = bf16[16,512,720]{1,2,0:T(8,128)(2,1)} async-done(((bf16[16,512,720]{1,2,0:T(8,128)(2,1)}), bf16[16,512,720]{1,2,0:T(8,128)(2,1)}, u32[]{:S(2)}, u32[]{:S(2)}) %all-to-all-start) | async-done | bytes 11796512 | tf_op jit(solution)/shard_map/all_to_all | solution.py:96
  517.8 7.6 %all-to-all-start.1 = ((bf16[2,16,16,2304]{3,2,0,1:T(8,128)(2,1)}), bf16[2,16,16,2304]{3,2,0,1:T(8,128)(2,1)}, u32[]{:S(2)}, u32[]{:S(2)}) async-start(bf16[2,16,16,2304]{3,2,0,1:T(8,128)(2,1)} %bitcast.43), calls=%async_computation.3 | async-start | bytes 4718592 | tf_op jit(solution)/shard_map/all_to_all | solution.py:34
  525.4 19.8 %copy.64 = bf16[16,512,720]{1,0,2:T(8,128)(2,1)} copy(bf16[16,512,720]{1,2,0:T(8,128)(2,1)} %all-to-all-done) | data formatting | bytes 23592960 | tf_op jit(solution)/shard_map/all_to_all | solution.py:96
  545.3 18.0 %reshape_reshape.3 = bf16[8,1024,720]{1,0,2:T(8,128)(2,1)} reshape(bf16[16,512,720]{1,0,2:T(8,128)(2,1)} %copy.64) | data formatting | bytes 23592960 | tf_op jit(solution)/shard_map/reshape;reshape | solution.py:9
  563.3 21.7 %fusion = f32[8,1024,144]{2,1,0:T(8,128)} fusion(bf16[8,720,144]{1,2,0:T(8,128)(2,1)S(1)} %copy-done, bf16[8,1024,720]{1,0,2:T(8,128)(2,1)} %reshape_reshape.3), kind=kOutput, calls=%fused_computation.11 | convolution fusion | flops 1698693120 | bytes 18173952 | tf_op jit(solution)/shard_map/reshape | solution.py:11
  585.0 11.9 %gather_fusion.3 = f32[2048,144]{1,0:T(8,128)} fusion(f32[8192,144]{1,0:T(8,128)} %bitcast.39, s32[2048]{0:T(1024)S(1)} %get-tuple-element.20), kind=kCustom, calls=%fused_computation.3 | custom fusion | bytes 2367488 | tf_op jit(solution)/shard_map/gather | solution.py:100
  596.9 12.0 %gather_fusion.2 = f32[2048,144]{1,0:T(8,128)} fusion(f32[8192,144]{1,0:T(8,128)} %bitcast.40, s32[2048]{0:T(1024)S(1)} %get-tuple-element.21), kind=kCustom, calls=%fused_computation.2 | custom fusion | bytes 2367488 | tf_op jit(solution)/shard_map/gather | solution.py:100
  608.9 3.4 add_convert_fusion
  613.0 3.2 copy.69
  616.3 3.8 gather_fusion.5
  620.0 3.2 copy.71
  623.3 30.3 %reduce-scatter.5.cloned.1.call-done = bf16[256,144]{1,0:T(8,128)(2,1)} async-done(((bf16[2048,144]{1,0:T(8,128)(2,1)}), bf16[256,144]{1,0:T(8,128)(2,1)}) %reduce-scatter.5.cloned.1.call-update) | async-done | bytes 73744 | tf_op jit(solution)/shard_map/reduce_scatter | solution.py:101
  653.6 1.6 copy.70
  (57 shorter events, 7.7 us)
Async XLA Ops:
  7.2 556.1 %copy-start = (bf16[8,720,144]{1,2,0:T(8,128)(2,1)S(1)}, bf16[8,720,144]{1,2,0:T(8,128)(2,1)}, u32[]{:S(2)}) copy-start(bf16[8,720,144]{1,2,0:T(8,128)(2,1)} %param.13) | copy-start | bytes 4976644
  7.2 310.9 %reduce-scatter.3.cloned.1.call-start = ((), (), s32[]{:S(2)}) async-start(), calls=%async_computation.4 | async-start | bytes 25067520 | tf_op jit(solution)/shard_map/reduce_scatter | solution.py:84
  14.4 20.3 %copy-start.3 = (bf16[256,144]{0,1:T(8,128)(2,1)S(1)}, bf16[256,144]{0,1:T(8,128)(2,1)}, u32[]{:S(2)}) copy-start(bf16[256,144]{0,1:T(8,128)(2,1)} %param.10) | copy-start | bytes 221188
  135.0 0.7 copy-start.4
  325.7 5.0 copy-start.2
  325.7 5.7 copy-start.5
  325.7 5.8 copy-start.6
  325.7 192.0 %all-to-all-start = ((bf16[16,512,720]{1,2,0:T(8,128)(2,1)}), bf16[16,512,720]{1,2,0:T(8,128)(2,1)}, u32[]{:S(2)}, u32[]{:S(2)}) async-start(bf16[16,512,720]{1,2,0:T(8,128)(2,1)} %stack.2), calls=%async_computation.1 | async-start | bytes 23592960 | tf_op jit(solution)/shard_map/all_to_all | solution.py:96
  338.3 3.9 copy-start.1
  517.8 95.3 %all-to-all-start.1 = ((bf16[2,16,16,2304]{3,2,0,1:T(8,128)(2,1)}), bf16[2,16,16,2304]{3,2,0,1:T(8,128)(2,1)}, u32[]{:S(2)}, u32[]{:S(2)}) async-start(bf16[2,16,16,2304]{3,2,0,1:T(8,128)(2,1)} %bitcast.43), calls=%async_computation.3 | async-start | bytes 4718592 | tf_op jit(solution)/shard_map/all_to_all | solution.py:34
  525.4 128.2 %reduce-scatter.5.cloned.1.call-start = ((), (), s32[]{:S(2)}) async-start(), calls=%async_computation.5 | async-start | bytes 1179648 | tf_op jit(solution)/shard_map/reduce_scatter | solution.py:101
Sparse Core Ops, SparseCore 0:
  135.1 182.8 reduce-scatter.2
  612.5 41.0 reduce-scatter.4
